TPU v7x, 256 devices: a whole 4x4x8 slice. The times are simulated.
256 devices in a mesh: section: 4 (over x), seq: 16 (over z, y_hi), tp: 4 (over y_lo, core).
Axes of the slice: x: 4, y: 4 (y_hi: 2, y_lo: 2; y = y_hi * 2 + y_lo), z: 8, core: 2. Of those that a mesh axis runs over, the one named last changes fastest.
Arguments:
- queries: bfloat16 [4, 4096, 8192], P('section', 'seq', 'tp'), may hold values from -135 to 135
- upstream: bfloat16 [4, 4096, 8192], P('section', 'seq', 'tp'), may hold values from -48 to 48
- shared_kv: bfloat16 [2, 4096, 1024], P(None, ('seq', 'tp')), may hold values from -5 to 5
Outputs:
- d_queries: bfloat16 [4, 4096, 8192], P('section', 'seq', 'tp')
- d_shared_kv: float32 [2, 4096, 1024], P(None, ('seq', 'tp'))
All inputs are finite; a program needn't handle non-finite values.
Results may differ from a plain program's by a relative error of at most 0.0098.
Values may be sent and summed in bfloat16 or wider, within the bound.
No kernel may reach another device: no remote copies, remote signals or barrier semaphores. Data moves between devices by JAX's collectives and lax.ppermute only.
A program may use at most 128 MiB of HBM per device.

v0:
```python
import math
import jax
import jax.numpy as jnp
from jax import lax
from jax.sharding import PartitionSpec as P

QH = 64
KVH = 8
HD = 128
WINDOW = 1024


def shifted(value, axis, by):
    peers = lax.axis_size(axis)
    pairs = [(i, i + by) for i in range(peers) if 0 <= i + by < peers]
    return lax.ppermute(value, axis, pairs)


def head_grads(query_block, grad_block, keys_head, values_head, allowed, score_scale):
    scores = (
        jnp.einsum("rgd,ed->gre", query_block, keys_head, preferred_element_type=jnp.float32)
        * score_scale
    )
    masked = jnp.where(allowed[None], scores, -jnp.inf)
    highest = jnp.max(masked, axis=-1, keepdims=True)
    weights = jnp.exp(masked - highest)
    probs = weights / jnp.sum(weights, axis=-1, keepdims=True)
    probs_b = probs.astype(jnp.bfloat16)
    attn_out = jnp.einsum("gre,ed->rgd", probs_b, values_head, preferred_element_type=jnp.float32)
    delta = jnp.sum(grad_block.astype(jnp.float32) * attn_out, axis=-1)
    dprobs = jnp.einsum("rgd,ed->gre", grad_block, values_head, preferred_element_type=jnp.float32)
    dscores = probs * (dprobs - jnp.transpose(delta)[:, :, None])
    dscores_b = dscores.astype(jnp.bfloat16)
    grad_query = (
        jnp.einsum("gre,ed->rgd", dscores_b, keys_head, preferred_element_type=jnp.float32)
        * score_scale
    )
    grad_key = (
        jnp.einsum("gre,rgd->ed", dscores_b, query_block, preferred_element_type=jnp.float32)
        * score_scale
    )
    grad_value = jnp.einsum("gre,rgd->ed", probs_b, grad_block, preferred_element_type=jnp.float32)
    return (grad_query, grad_key, grad_value)


def body(queries, upstream, shared_kv):
    local_kv = lax.all_to_all(shared_kv, "tp", split_axis=2, concat_axis=1, tiled=True)
    tok_rows = local_kv.shape[1]
    kv_cols = local_kv.shape[2]
    head_size = HD
    local_kv_heads = kv_cols // head_size
    group_size = QH // KVH
    block_heads = max(1, group_size // 2)
    span_blocks = WINDOW // tok_rows
    score_scale = 1.0 / math.sqrt(head_size)
    earlier = [shifted(local_kv, "seq", span_blocks - offset) for offset in range(span_blocks)]
    extended = jnp.concatenate(earlier + [local_kv], axis=1)
    ext_rows = extended.shape[1]
    position = lax.axis_index("seq")
    row_ids = lax.broadcasted_iota(jnp.int32, (tok_rows, ext_rows), 0)
    key_ids = lax.broadcasted_iota(jnp.int32, (tok_rows, ext_rows), 1)
    allowed = (
        (key_ids >= row_ids + 1)
        & (key_ids <= row_ids + WINDOW)
        & (position * tok_rows - WINDOW + key_ids >= 0)
    )
    query_heads = queries.reshape(tok_rows, -1, head_size)
    grad_heads = upstream.reshape(tok_rows, -1, head_size)
    query_parts = []
    key_parts = []
    value_parts = []
    for kv_head in range(local_kv_heads):
        keys_head = extended[0, :, kv_head * head_size : (kv_head + 1) * head_size]
        values_head = extended[1, :, kv_head * head_size : (kv_head + 1) * head_size]
        key_total = jnp.zeros((ext_rows, head_size), jnp.float32)
        value_total = jnp.zeros((ext_rows, head_size), jnp.float32)
        for first_head in range(kv_head * group_size, (kv_head + 1) * group_size, block_heads):
            query_block = query_heads[:, first_head : first_head + block_heads]
            grad_block = grad_heads[:, first_head : first_head + block_heads]
            grad_query, grad_key, grad_value = head_grads(
                query_block, grad_block, keys_head, values_head, allowed, score_scale
            )
            query_parts.append(grad_query)
            key_total = key_total + grad_key
            value_total = value_total + grad_value
        key_parts.append(key_total)
        value_parts.append(value_total)
    d_queries = jnp.concatenate(query_parts, axis=1).reshape(1, tok_rows, -1).astype(jnp.bfloat16)
    grad_ext = jnp.stack([jnp.concatenate(key_parts, axis=1), jnp.concatenate(value_parts, axis=1)])
    own_rows = grad_ext[:, span_blocks * tok_rows :, :]
    for offset in range(span_blocks):
        own_rows = own_rows + shifted(
            grad_ext[:, offset * tok_rows : (offset + 1) * tok_rows, :].astype(jnp.bfloat16),
            "seq",
            offset - span_blocks,
        ).astype(jnp.float32)
    summed = lax.psum(own_rows, "section")
    d_shared_kv = lax.all_to_all(summed, "tp", split_axis=1, concat_axis=2, tiled=True)
    return (d_queries, d_shared_kv)


def solution(mesh):
    in_specs = (P("section", "seq", "tp"), P("section", "seq", "tp"), P(None, ("seq", "tp"), None))
    out_specs = (P("section", "seq", "tp"), P(None, ("seq", "tp"), None))
    return jax.shard_map(body, mesh=mesh, in_specs=in_specs, out_specs=out_specs, check_vma=False)
```

profile of v0, /device:TPU:1, one launch (start us, length us, event | category | flops | bytes accessed | tf_op | source)
XLA Modules:
  0.0 228.5 jit_solution(4104117547018688944)
XLA Ops:
  7.2 1.4 copy.143
  8.5 1.1 reshape.105
  9.6 6.6 %all-to-all-start = ((bf16[4,2,16384]{2,1,0:T(2,128)(2,1)}), bf16[4,2,16384]{2,1,0:T(2,128)(2,1)S(1)}, u32[]{:S(2)}, u32[]{:S(2)}) async-start(bf16[4,2,16384]{2,1,0:T(2,128)(2,1)} %reshape.105), calls=%async_computation | async-start | bytes 524288 | tf_op jit(solution)/shard_map/all_to_all | solution.py:47
  16.2 5.0 %all-to-all-done = bf16[4,2,16384]{2,1,0:T(2,128)(2,1)S(1)} async-done(((bf16[4,2,16384]{2,1,0:T(2,128)(2,1)}), bf16[4,2,16384]{2,1,0:T(2,128)(2,1)S(1)}, u32[]{:S(2)}, u32[]{:S(2)}) %all-to-all-start) | async-done | bytes 262176 | tf_op jit(solution)/shard_map/all_to_all | solution.py:47
  21.6 1.0 copy.144
  22.6 3.9 %collective-permute-start = (bf16[2,256,256]{2,1,0:T(8,128)(2,1)}, bf16[2,256,256]{2,1,0:T(8,128)(2,1)}, u32[]{:S(2)}, u32[]{:S(2)}) collective-permute-start(bf16[2,256,256]{2,1,0:T(8,128)(2,1)} %bitcast.2), channel_id=1, source_target_pairs={{0,16},{4,20},{8,24},{12,28},{16,32},{20,36},{24,40},{28,44},{32,4... | collective-permute-start | bytes 786440 | tf_op jit(solution)/shard_map/ppermute | solution.py:16
  26.5 1.1 fusion.28
  28.2 4.3 %collective-permute-start.2 = (bf16[2,256,256]{2,1,0:T(8,128)(2,1)}, bf16[2,256,256]{2,1,0:T(8,128)(2,1)}, u32[]{:S(2)}, u32[]{:S(2)}) collective-permute-start(bf16[2,256,256]{2,1,0:T(8,128)(2,1)} %bitcast.2), channel_id=1, source_target_pairs={{0,8},{4,12},{8,16},{12,20},{16,24},{20,28},{24,32},{28,36},{32,40... | collective-permute-start | bytes 786440 | tf_op jit(solution)/shard_map/ppermute | solution.py:16
  32.4 6.7 %collective-permute-start.1 = (bf16[2,256,256]{2,1,0:T(8,128)(2,1)}, bf16[2,256,256]{2,1,0:T(8,128)(2,1)}, u32[]{:S(2)}, u32[]{:S(2)}) collective-permute-start(bf16[2,256,256]{2,1,0:T(8,128)(2,1)} %bitcast.2), channel_id=1, source_target_pairs={{0,12},{4,16},{8,20},{12,24},{16,28},{20,32},{24,36},{28,40},{32,4... | collective-permute-start | bytes 786440 | tf_op jit(solution)/shard_map/ppermute | solution.py:16
  39.2 1.5 copy.145
  40.7 1.0 copy.240
  41.7 0.9 copy.244
  42.6 0.9 copy.242
  43.5 0.8 copy.246
  44.3 2.6 %collective-permute-start.3 = (bf16[2,256,256]{2,1,0:T(8,128)(2,1)}, bf16[2,256,256]{2,1,0:T(8,128)(2,1)S(1)}, u32[]{:S(2)}, u32[]{:S(2)}) collective-permute-start(bf16[2,256,256]{2,1,0:T(8,128)(2,1)} %bitcast.2), channel_id=1, source_target_pairs={{0,4},{4,8},{8,12},{12,16},{16,20},{20,24},{24,28},{28,32},{32,36}... | collective-permute-start | bytes 786440 | tf_op jit(solution)/shard_map/ppermute | solution.py:16
  46.9 1.0 constant_dynamic-update-slice_fusion.4
  47.9 1.0 constant_dynamic-update-slice_fusion.3
  48.9 1.0 constant_dynamic-update-slice_fusion.2
  49.9 1.0 collective-permute-done.3
  50.9 1.0 constant_dynamic-update-slice_fusion
  51.9 5.3 %exponential_reduce_fusion.3 = (f32[4,256]{1,0:T(4,128)S(1)}, f32[4,256,1280]{1,2,0:T(8,128)}) fusion(pred[256,1280]{0,1:T(8,128)(4,1)} %fusion.28, bf16[256,16,128]{0,2,1:T(8,128)(2,1)S(1)} %bitcast.227, bf16[2,1280,256]{2,1,0:T(8,128)(2,1)S(1)} %constant_dynamic-update-slice_fusion), kind=kOutput, calls=%fused_computation.31 | convolution fusion | flops 340788480 | bytes 6164480 | tf_op jit(solution)/shard_map/sub | solution.py:26
  57.1 5.1 %exponential_reduce_fusion.1 = (f32[4,256]{1,0:T(4,128)S(1)}, f32[4,256,1280]{1,2,0:T(8,128)}) fusion(pred[256,1280]{0,1:T(8,128)(4,1)} %fusion.28, bf16[256,16,128]{0,2,1:T(8,128)(2,1)S(1)} %bitcast.228, bf16[2,1280,256]{2,1,0:T(8,128)(2,1)S(1)} %constant_dynamic-update-slice_fusion), kind=kOutput, calls=%fused_computation.27 | convolution fusion | flops 340788480 | bytes 6164480 | tf_op jit(solution)/shard_map/sub | solution.py:26
  62.3 5.1 %exponential_reduce_fusion.2 = (f32[4,256]{1,0:T(4,128)S(1)}, f32[4,256,1280]{1,2,0:T(8,128)}) fusion(pred[256,1280]{0,1:T(8,128)(4,1)} %fusion.28, bf16[256,16,128]{0,2,1:T(8,128)(2,1)S(1)} %bitcast.229, bf16[2,1280,256]{2,1,0:T(8,128)(2,1)S(1)} %constant_dynamic-update-slice_fusion), kind=kOutput, calls=%fused_computation.29 | convolution fusion | flops 340788480 | bytes 6164480 | tf_op jit(solution)/shard_map/sub | solution.py:26
  67.4 5.1 %exponential_reduce_fusion = (f32[4,256]{1,0:T(4,128)S(1)}, f32[4,256,1280]{1,2,0:T(8,128)}) fusion(pred[256,1280]{0,1:T(8,128)(4,1)} %fusion.28, bf16[256,16,128]{0,2,1:T(8,128)(2,1)S(1)} %bitcast.230, bf16[2,1280,256]{2,1,0:T(8,128)(2,1)S(1)} %constant_dynamic-update-slice_fusion), kind=kOutput, calls=%fused_computation.25 | convolution fusion | flops 340788480 | bytes 6164480 | tf_op jit(solution)/shard_map/sub | solution.py:26
  72.5 4.0 %fusion.23 = bf16[4,256,1280]{1,2,0:T(8,128)(2,1)S(1)} fusion(f32[4,256]{1,0:T(4,128)S(1)} %get-tuple-element.24, f32[4,256,1280]{1,2,0:T(8,128)} %get-tuple-element.25), kind=kLoop, calls=%fused_computation.50 | loop fusion | flops 2621440 | bytes 7868416 | tf_op jit(solution)/shard_map/convert_element_type | solution.py:28
  76.5 1.0 convolution_bitcast_fusion.3
  77.5 1.3 fusion.37
  78.8 1.1 fusion.15
  79.9 1.0 convolution_bitcast_fusion.7
  81.2 1.6 fusion.25
  82.9 1.0 convolution_bitcast_fusion.1
  83.9 1.3 fusion.39
  85.2 1.1 fusion.11
  86.3 1.0 convolution_bitcast_fusion.5
  87.3 0.6 copy-done.2
  87.9 0.7 slice-done.3
  88.6 1.4 fusion.24
  90.0 1.3 fusion.38
  91.3 1.0 fusion.18
  92.3 1.1 fusion.13
  93.5 1.2 slice-done
  94.7 1.0 slice-done.1
  95.7 1.4 fusion.26
  97.2 1.3 fusion.40
  98.5 1.0 fusion.17
  99.8 2.5 %fusion.9 = bf16[4,256,1280]{1,2,0:T(8,128)(2,1)S(1)} fusion(f32[4,256]{1,0:T(4,128)S(1)} %bitcast.240, f32[4,256]{1,0:T(4,128)S(1)} %get-tuple-element.18, f32[4,256,1280]{1,2,0:T(8,128)S(1)} %bitcast.220, bf16[2,1280,256]{2,1,0:T(8,128)(2,1)S(1)} %copy-done.5, bf16[256,16,128]{0,2,1:T(8,128)(2,1)} %bitcast.218), kind=kOutput, calls=%fused_computation.10 | convolution fusion | flops 340787200 | bytes 8462336 | tf_op jit(solution)/shard_map/rgd,ed->gre/dot_general | solution.py:31
  102.3 1.0 fusion.22
  103.4 1.0 fusion.20
  104.7 1.3 collective-permute-start.4
  106.0 1.3 collective-permute-start.7
  107.3 1.3 collective-permute-start.6
  108.6 1.3 collective-permute-start.5
  110.5 22.5 %collective-permute-done.4 = bf16[2,256,256]{1,2,0:T(8,128)(2,1)S(1)} collective-permute-done((bf16[2,256,256]{1,2,0:T(8,128)(2,1)S(1)}, bf16[2,256,256]{1,2,0:T(8,128)(2,1)S(1)}, u32[]{:S(2)}, u32[]{:S(2)}) %collective-permute-start.4) | collective-permute-done | bytes 262176 | tf_op jit(solution)/shard_map/ppermute | solution.py:16
  133.0 6.1 %collective-permute-done.5 = bf16[2,256,256]{1,2,0:T(8,128)(2,1)S(1)} collective-permute-done((bf16[2,256,256]{1,2,0:T(8,128)(2,1)S(1)}, bf16[2,256,256]{1,2,0:T(8,128)(2,1)S(1)}, u32[]{:S(2)}, u32[]{:S(2)}) %collective-permute-start.5) | collective-permute-done | bytes 262176 | tf_op jit(solution)/shard_map/ppermute | solution.py:16
  139.1 1.0 fusion.49
  140.1 3.2 %fusion.42 = bf16[256,4,128]{0,2,1:T(8,128)(2,1)} fusion(bf16[4,256,1280]{1,2,0:T(8,128)(2,1)} %copy-done.2, bf16[2,1280,256]{2,1,0:T(8,128)(2,1)} %copy-done.4), kind=kOutput, calls=%fused_computation.81 | convolution fusion | flops 335806464 | bytes 3211264 | tf_op jit(solution)/shard_map/gre,ed->rgd/dot_general | solution.py:35
  143.3 2.2 fusion.43
  145.5 59.1 %all-reduce.2.cloned.1.call-done = f32[2,256,256]{1,2,0:T(8,128)} async-done(((f32[2,256,256]{1,2,0:T(8,128)}), f32[2,256,256]{1,2,0:T(8,128)}) %all-reduce.2.cloned.1.call-update) | async-done | bytes 524304 | tf_op jit(solution)/shard_map/psum | solution.py:97
  204.6 2.0 copy.191
  206.6 6.3 %all-to-all-start.1 = ((f32[2,256,256]{2,0,1:T(2,128)}), f32[2,256,256]{2,0,1:T(2,128)S(1)}, u32[]{:S(2)}, u32[]{:S(2)}) async-start(f32[2,256,256]{2,0,1:T(2,128)} %copy.191), calls=%async_computation.1 | async-start | bytes 1048576 | tf_op jit(solution)/shard_map/all_to_all | solution.py:98
  213.0 1.6 fusion.41
  214.7 1.4 copy.194
  216.1 4.7 %all-to-all-done.1 = f32[2,256,256]{2,0,1:T(2,128)S(1)} async-done(((f32[2,256,256]{2,0,1:T(2,128)}), f32[2,256,256]{2,0,1:T(2,128)S(1)}, u32[]{:S(2)}, u32[]{:S(2)}) %all-to-all-start.1) | async-done | bytes 524320 | tf_op jit(solution)/shard_map/all_to_all | solution.py:98
  220.8 0.8 copy.247
  (66 shorter events, 2.9 us)
Async XLA Ops:
  7.2 20.5 %copy-start.12 = (bf16[1,256,2048]{2,1,0:T(8,128)(2,1)S(1)}, bf16[1,256,2048]{2,1,0:T(8,128)(2,1)}, u32[]{:S(2)}) copy-start(bf16[1,256,2048]{2,1,0:T(8,128)(2,1)} %param.4) | copy-start | bytes 3145732
  9.6 11.6 %all-to-all-start = ((bf16[4,2,16384]{2,1,0:T(2,128)(2,1)}), bf16[4,2,16384]{2,1,0:T(2,128)(2,1)S(1)}, u32[]{:S(2)}, u32[]{:S(2)}) async-start(bf16[4,2,16384]{2,1,0:T(2,128)(2,1)} %reshape.105), calls=%async_computation | async-start | bytes 524288 | tf_op jit(solution)/shard_map/all_to_all | solution.py:47
  16.2 188.4 %all-reduce.2.cloned.1.call-start = ((), (), s32[]{:S(2)}) async-start(), calls=%async_computation.2 | async-start | bytes 1048576 | tf_op jit(solution)/shard_map/psum | solution.py:97
  22.6 24.3 %collective-permute-start = (bf16[2,256,256]{2,1,0:T(8,128)(2,1)}, bf16[2,256,256]{2,1,0:T(8,128)(2,1)}, u32[]{:S(2)}, u32[]{:S(2)}) collective-permute-start(bf16[2,256,256]{2,1,0:T(8,128)(2,1)} %bitcast.2), channel_id=1, source_target_pairs={{0,16},{4,20},{8,24},{12,28},{16,32},{20,36},{24,40},{28,44},{32,4... | collective-permute-start | bytes 786440 | tf_op jit(solution)/shard_map/ppermute | solution.py:16
  28.2 70.3 %copy-start.3 = (bf16[1,256,2048]{1,2,0:T(8,128)(2,1)}, bf16[1,256,2048]{1,2,0:T(8,128)(2,1)S(1)}, u32[]{:S(2)}) copy-start(bf16[1,256,2048]{1,2,0:T(8,128)(2,1)S(1)} %copy.147) | copy-start | bytes 3145732
  28.2 20.7 %collective-permute-start.2 = (bf16[2,256,256]{2,1,0:T(8,128)(2,1)}, bf16[2,256,256]{2,1,0:T(8,128)(2,1)}, u32[]{:S(2)}, u32[]{:S(2)}) collective-permute-start(bf16[2,256,256]{2,1,0:T(8,128)(2,1)} %bitcast.2), channel_id=1, source_target_pairs={{0,8},{4,12},{8,16},{12,20},{16,24},{20,28},{24,32},{28,36},{32,40... | collective-permute-start | bytes 786440 | tf_op jit(solution)/shard_map/ppermute | solution.py:16
  32.4 15.5 %collective-permute-start.1 = (bf16[2,256,256]{2,1,0:T(8,128)(2,1)}, bf16[2,256,256]{2,1,0:T(8,128)(2,1)}, u32[]{:S(2)}, u32[]{:S(2)}) collective-permute-start(bf16[2,256,256]{2,1,0:T(8,128)(2,1)} %bitcast.2), channel_id=1, source_target_pairs={{0,12},{4,16},{8,20},{12,24},{16,28},{20,32},{24,36},{28,40},{32,4... | collective-permute-start | bytes 786440 | tf_op jit(solution)/shard_map/ppermute | solution.py:16
  40.7 45.6 %copy-start.6 = (bf16[1,256,2048]{1,2,0:T(8,128)(2,1)}, bf16[1,256,2048]{1,2,0:T(8,128)(2,1)S(1)}, u32[]{:S(2)}) copy-start(bf16[1,256,2048]{1,2,0:T(8,128)(2,1)S(1)} %copy.145) | copy-start | bytes 3145732
  44.3 6.6 %collective-permute-start.3 = (bf16[2,256,256]{2,1,0:T(8,128)(2,1)}, bf16[2,256,256]{2,1,0:T(8,128)(2,1)S(1)}, u32[]{:S(2)}, u32[]{:S(2)}) collective-permute-start(bf16[2,256,256]{2,1,0:T(8,128)(2,1)} %bitcast.2), channel_id=1, source_target_pairs={{0,4},{4,8},{8,12},{12,16},{16,20},{20,24},{24,28},{28,32},{32,36}... | collective-permute-start | bytes 786440 | tf_op jit(solution)/shard_map/ppermute | solution.py:16
  51.9 45.3 %copy-start.4 = (bf16[2,1280,256]{2,1,0:T(8,128)(2,1)}, bf16[2,1280,256]{2,1,0:T(8,128)(2,1)S(1)}, u32[]{:S(2)}) copy-start(bf16[2,1280,256]{2,1,0:T(8,128)(2,1)S(1)} %constant_dynamic-update-slice_fusion) | copy-start | bytes 3932164
  72.5 6.3 %slice-start.6 = ((s8[5242880]{0:T(1024)(128)(4,1)}), s8[4194304]{0:T(1024)(128)(4,1)S(1)}, s32[]{:S(2)}) async-start(s8[5242880]{0:T(1024)(128)(4,1)} %bitcast.225), calls=%async_computation.9 | async-start | bytes 8388608
  76.5 1.0 copy-start.11
  76.5 2.3 %slice-start.7 = ((s8[5242880]{0:T(1024)(128)(4,1)}), s8[1048576]{0:T(1024)(128)(4,1)S(1)}, s32[]{:S(2)}) async-start(s8[5242880]{0:T(1024)(128)(4,1)} %bitcast.225), calls=%async_computation.10 | async-start | bytes 2097152
  78.8 2.2 slice-start.4
  78.8 2.5 %slice-start.5 = ((s8[5242880]{0:T(1024)(128)(4,1)}), s8[1048576]{0:T(1024)(128)(4,1)S(1)}, s32[]{:S(2)}) async-start(s8[5242880]{0:T(1024)(128)(4,1)} %bitcast.223), calls=%async_computation.8 | async-start | bytes 2097152
  82.9 1.0 copy-start.10
  85.2 2.7 %slice-start.2 = ((s8[5242880]{0:T(1024)(128)(4,1)}), s8[4194304]{0:T(1024)(128)(4,1)S(1)}, s32[]{:S(2)}) async-start(s8[5242880]{0:T(1024)(128)(4,1)} %bitcast.221), calls=%async_computation.5 | async-start | bytes 8388608
  85.2 3.4 %slice-start.3 = ((s8[5242880]{0:T(1024)(128)(4,1)}), s8[1048576]{0:T(1024)(128)(4,1)S(1)}, s32[]{:S(2)}) async-start(s8[5242880]{0:T(1024)(128)(4,1)} %bitcast.221), calls=%async_computation.6 | async-start | bytes 2097152
  86.3 1.6 copy-start.2
  88.6 1.4 copy-start.9
  92.3 2.4 %slice-start = ((s8[5242880]{0:T(1024)(128)(4,1)}), s8[4194304]{0:T(1024)(128)(4,1)S(1)}, s32[]{:S(2)}) async-start(s8[5242880]{0:T(1024)(128)(4,1)} %bitcast.219), calls=%async_computation.3 | async-start | bytes 8388608
  92.3 3.4 %slice-start.1 = ((s8[5242880]{0:T(1024)(128)(4,1)}), s8[1048576]{0:T(1024)(128)(4,1)S(1)}, s32[]{:S(2)}) async-start(s8[5242880]{0:T(1024)(128)(4,1)} %bitcast.219), calls=%async_computation.4 | async-start | bytes 2097152
  93.5 8.8 %copy-start = (bf16[4,256,1280]{1,2,0:T(8,128)(2,1)}, bf16[4,256,1280]{1,2,0:T(8,128)(2,1)S(1)}, u32[]{:S(2)}) copy-start(bf16[4,256,1280]{1,2,0:T(8,128)(2,1)S(1)} %fusion.13) | copy-start | bytes 7864324
  95.7 1.4 copy-start.8
  98.5 1.3 copy-start.5
  99.8 2.5 %copy-start.7 = (bf16[1,256,2048]{1,2,0:T(8,128)(2,1)S(1)}, bf16[1,256,2048]{1,2,0:T(8,128)(2,1)}, u32[]{:S(2)}) copy-start(bf16[1,256,2048]{1,2,0:T(8,128)(2,1)} %copy-done.6) | copy-start | bytes 3145732
  104.7 28.2 %collective-permute-start.4 = (bf16[2,256,256]{1,2,0:T(8,128)(2,1)S(1)}, bf16[2,256,256]{1,2,0:T(8,128)(2,1)S(1)}, u32[]{:S(2)}, u32[]{:S(2)}) collective-permute-start(bf16[2,256,256]{1,2,0:T(8,128)(2,1)S(1)} %get-tuple-element.10), channel_id=1, source_target_pairs={{16,0},{20,4},{24,8},{28,12},{32,16},{36,20},{40,24},{44,28},{48,3... | collective-permute-start | bytes 786440 | tf_op jit(solution)/shard_map/ppermute | solution.py:16
  106.0 26.9 %collective-permute-start.7 = (bf16[2,256,256]{1,2,0:T(8,128)(2,1)S(1)}, bf16[2,256,256]{1,2,0:T(8,128)(2,1)S(1)}, u32[]{:S(2)}, u32[]{:S(2)}) collective-permute-start(bf16[2,256,256]{1,2,0:T(8,128)(2,1)S(1)} %get-tuple-element.11), channel_id=1, source_target_pairs={{4,0},{8,4},{12,8},{16,12},{20,16},{24,20},{28,24},{32,28},{36,32}... | collective-permute-start | bytes 786440 | tf_op jit(solution)/shard_map/ppermute | solution.py:16
  107.3 25.6 %collective-permute-start.6 = (bf16[2,256,256]{1,2,0:T(8,128)(2,1)S(1)}, bf16[2,256,256]{1,2,0:T(8,128)(2,1)S(1)}, u32[]{:S(2)}, u32[]{:S(2)}) collective-permute-start(bf16[2,256,256]{1,2,0:T(8,128)(2,1)S(1)} %get-tuple-element.12), channel_id=1, source_target_pairs={{8,0},{12,4},{16,8},{20,12},{24,16},{28,20},{32,24},{36,28},{40,32... | collective-permute-start | bytes 786440 | tf_op jit(solution)/shard_map/ppermute | solution.py:16
  108.6 30.4 %collective-permute-start.5 = (bf16[2,256,256]{1,2,0:T(8,128)(2,1)S(1)}, bf16[2,256,256]{1,2,0:T(8,128)(2,1)S(1)}, u32[]{:S(2)}, u32[]{:S(2)}) collective-permute-start(bf16[2,256,256]{1,2,0:T(8,128)(2,1)S(1)} %get-tuple-element.13), channel_id=1, source_target_pairs={{12,0},{16,4},{20,8},{24,12},{28,16},{32,20},{36,24},{40,28},{44,3... | collective-permute-start | bytes 786440 | tf_op jit(solution)/shard_map/ppermute | solution.py:16
  140.1 3.3 %copy-start.1 = (bf16[4,256,1280]{1,2,0:T(8,128)(2,1)S(1)}, bf16[4,256,1280]{1,2,0:T(8,128)(2,1)}, u32[]{:S(2)}) copy-start(bf16[4,256,1280]{1,2,0:T(8,128)(2,1)} %copy-done) | copy-start | bytes 7864324
  206.6 14.2 %all-to-all-start.1 = ((f32[2,256,256]{2,0,1:T(2,128)}), f32[2,256,256]{2,0,1:T(2,128)S(1)}, u32[]{:S(2)}, u32[]{:S(2)}) async-start(f32[2,256,256]{2,0,1:T(2,128)} %copy.191), calls=%async_computation.1 | async-start | bytes 1048576 | tf_op jit(solution)/shard_map/all_to_all | solution.py:98
  213.0 1.6 copy-start.13
  213.0 1.6 copy-start.14
Sparse Core Ops, SparseCore 0:
  140.2 64.3 all-reduce.1
where the time goes:
time: 229 us
  waiting for transfers between devices  98.4 us (43%)
  matrix products  47 us (21%)
  starting transfers between devices  35.5 us (16%)
  local copies, waits for them, and re-layouts  22.1 us (10%)
  between operations  14.6 us (6%)
  other arithmetic  11 us (5%)
    psum x1, waiting for transfers between devices, body(): summed = lax.psum(own_rows, 'section')  59.1 us
    ppermute x8, waiting for transfers between devices, shifted(): return lax.ppermute(value, axis, pairs)  29.6 us
    ppermute x8, starting transfers between devices, shifted(): return lax.ppermute(value, axis, pairs)  22.6 us
    sub x4, matrix products, head_grads(): weights = jnp.exp(masked - highest)  20.6 us
    unnamed x61, local copies, waits for them, and re-layouts  17.1 us
    convert_element_type x4, other arithmetic, head_grads(): probs_b = probs.astype(jnp.bfloat16)  8.43 us
    dot_general x4, matrix products, head_grads(): jnp.einsum('gre,ed->rgd', dscores_b, keys_head, preferred_element_type=jn...  7.58 us
    all_to_all x1, starting transfers between devices, body(): lax.all_to_all(shared_kv, 'tp', split_axis=2, concat_axis=1, tiled=True)  6.57 us
  transfers between devices with their start and end apart: 11, of which 6 were waited for; matrix products, arithmetic and copies ran while one was open for 8% of the time, Pallas kernels for 0%

commit v1 on v0

--- a/solution.py
+++ b/solution.py
@@ -94,7 +94,7 @@
             "seq",
             offset - span_blocks,
         ).astype(jnp.float32)
-    summed = lax.psum(own_rows, "section")
+    summed = jnp.sum(lax.all_gather(own_rows, "section"), axis=0)
     d_shared_kv = lax.all_to_all(summed, "tp", split_axis=1, concat_axis=2, tiled=True)
     return (d_queries, d_shared_kv)
 

time: 229 us -> 216 us (0.943)
  waiting for transfers between devices: 98.4 us -> 83.7 us
    psum x1 -> x0, waiting for transfers between devices: 59.1 us -> none  [body(): summed = lax.psum(own_rows, 'section')]
    all_gather x0 -> x1, waiting for transfers between devices: none -> 43.8 us  [body(): summed = jnp.sum(lax.all_gather(own_rows, 'section'), axis=0)]
  transfers between devices with their start and end apart: 11 -> 11, of which waited for: 6 -> 6; matrix products, arithmetic and copies ran while one was open for 8% -> 10% of each run, Pallas kernels for 0% -> 0%
where the time goes in v1:
time: 216 us
  waiting for transfers between devices  83.7 us (39%)
  matrix products  48.9 us (23%)
  starting transfers between devices  33.5 us (16%)
  local copies, waits for them, and re-layouts  22.8 us (11%)
  between operations  14.6 us (7%)
  other arithmetic  12 us (6%)
    all_gather x1, waiting for transfers between devices, body(): summed = jnp.sum(lax.all_gather(own_rows, 'section'), axis=0)  43.8 us
    ppermute x8, waiting for transfers between devices, shifted(): return lax.ppermute(value, axis, pairs)  30.2 us
    ppermute x8, starting transfers between devices, shifted(): return lax.ppermute(value, axis, pairs)  22.6 us
    sub x4, matrix products, head_grads(): weights = jnp.exp(masked - highest)  20.6 us
    unnamed x61, local copies, waits for them, and re-layouts  17.7 us
    dot_general x4, matrix products, head_grads(): jnp.einsum('gre,ed->rgd', dscores_b, keys_head, preferred_element_type=jn...  9.44 us
    convert_element_type x4, other arithmetic, head_grads(): probs_b = probs.astype(jnp.bfloat16)  8.43 us
    all_to_all x1, starting transfers between devices, body(): lax.all_to_all(shared_kv, 'tp', split_axis=2, concat_axis=1, tiled=True)  6.57 us
  transfers between devices with their start and end apart: 11, of which 6 were waited for; matrix products, arithmetic and copies ran while one was open for 10% of the time, Pallas kernels for 0%

profile of v1, /device:TPU:1, one launch (start us, length us, event | category | flops | bytes accessed | tf_op | source)
XLA Modules:
  0.0 215.5 jit_solution(13922902531498575796)
XLA Ops:
  7.2 1.4 copy.140
  8.5 1.1 reshape.106
  9.6 6.6 %all-to-all-start = ((bf16[4,2,16384]{2,1,0:T(2,128)(2,1)}), bf16[4,2,16384]{2,1,0:T(2,128)(2,1)S(1)}, u32[]{:S(2)}, u32[]{:S(2)}) async-start(bf16[4,2,16384]{2,1,0:T(2,128)(2,1)} %reshape.106), calls=%async_computation | async-start | bytes 524288 | tf_op jit(solution)/shard_map/all_to_all | solution.py:47
  16.2 5.0 %all-to-all-done = bf16[4,2,16384]{2,1,0:T(2,128)(2,1)S(1)} async-done(((bf16[4,2,16384]{2,1,0:T(2,128)(2,1)}), bf16[4,2,16384]{2,1,0:T(2,128)(2,1)S(1)}, u32[]{:S(2)}, u32[]{:S(2)}) %all-to-all-start) | async-done | bytes 262176 | tf_op jit(solution)/shard_map/all_to_all | solution.py:47
  21.6 1.0 copy.141
  22.6 3.9 %collective-permute-start = (bf16[2,256,256]{2,1,0:T(8,128)(2,1)}, bf16[2,256,256]{2,1,0:T(8,128)(2,1)}, u32[]{:S(2)}, u32[]{:S(2)}) collective-permute-start(bf16[2,256,256]{2,1,0:T(8,128)(2,1)} %bitcast.2), channel_id=1, source_target_pairs={{0,16},{4,20},{8,24},{12,28},{16,32},{20,36},{24,40},{28,44},{32,4... | collective-permute-start | bytes 786440 | tf_op jit(solution)/shard_map/ppermute | solution.py:16
  26.5 1.1 fusion.28
  28.2 4.3 %collective-permute-start.2 = (bf16[2,256,256]{2,1,0:T(8,128)(2,1)}, bf16[2,256,256]{2,1,0:T(8,128)(2,1)}, u32[]{:S(2)}, u32[]{:S(2)}) collective-permute-start(bf16[2,256,256]{2,1,0:T(8,128)(2,1)} %bitcast.2), channel_id=1, source_target_pairs={{0,8},{4,12},{8,16},{12,20},{16,24},{20,28},{24,32},{28,36},{32,40... | collective-permute-start | bytes 786440 | tf_op jit(solution)/shard_map/ppermute | solution.py:16
  32.4 6.7 %collective-permute-start.1 = (bf16[2,256,256]{2,1,0:T(8,128)(2,1)}, bf16[2,256,256]{2,1,0:T(8,128)(2,1)}, u32[]{:S(2)}, u32[]{:S(2)}) collective-permute-start(bf16[2,256,256]{2,1,0:T(8,128)(2,1)} %bitcast.2), channel_id=1, source_target_pairs={{0,12},{4,16},{8,20},{12,24},{16,28},{20,32},{24,36},{28,40},{32,4... | collective-permute-start | bytes 786440 | tf_op jit(solution)/shard_map/ppermute | solution.py:16
  39.2 1.5 copy.142
  40.7 1.0 copy.240
  41.7 0.9 copy.244
  42.6 0.9 copy.242
  43.5 0.8 copy.246
  44.3 2.6 %collective-permute-start.3 = (bf16[2,256,256]{2,1,0:T(8,128)(2,1)}, bf16[2,256,256]{2,1,0:T(8,128)(2,1)S(1)}, u32[]{:S(2)}, u32[]{:S(2)}) collective-permute-start(bf16[2,256,256]{2,1,0:T(8,128)(2,1)} %bitcast.2), channel_id=1, source_target_pairs={{0,4},{4,8},{8,12},{12,16},{16,20},{20,24},{24,28},{28,32},{32,36}... | collective-permute-start | bytes 786440 | tf_op jit(solution)/shard_map/ppermute | solution.py:16
  46.9 1.0 constant_dynamic-update-slice_fusion.4
  47.9 1.0 constant_dynamic-update-slice_fusion.3
  48.9 1.0 constant_dynamic-update-slice_fusion.2
  49.9 1.0 collective-permute-done.3
  50.9 1.0 constant_dynamic-update-slice_fusion
  51.9 5.3 %exponential_reduce_fusion.3 = (f32[4,256]{1,0:T(4,128)S(1)}, f32[4,256,1280]{1,2,0:T(8,128)}) fusion(pred[256,1280]{0,1:T(8,128)(4,1)} %fusion.28, bf16[256,16,128]{0,2,1:T(8,128)(2,1)S(1)} %bitcast.228, bf16[2,1280,256]{2,1,0:T(8,128)(2,1)S(1)} %constant_dynamic-update-slice_fusion), kind=kOutput, calls=%fused_computation.31 | convolution fusion | flops 340788480 | bytes 6164480 | tf_op jit(solution)/shard_map/sub | solution.py:26
  57.1 5.1 %exponential_reduce_fusion.1 = (f32[4,256]{1,0:T(4,128)S(1)}, f32[4,256,1280]{1,2,0:T(8,128)}) fusion(pred[256,1280]{0,1:T(8,128)(4,1)} %fusion.28, bf16[256,16,128]{0,2,1:T(8,128)(2,1)S(1)} %bitcast.229, bf16[2,1280,256]{2,1,0:T(8,128)(2,1)S(1)} %constant_dynamic-update-slice_fusion), kind=kOutput, calls=%fused_computation.27 | convolution fusion | flops 340788480 | bytes 6164480 | tf_op jit(solution)/shard_map/sub | solution.py:26
  62.3 5.1 %exponential_reduce_fusion.2 = (f32[4,256]{1,0:T(4,128)S(1)}, f32[4,256,1280]{1,2,0:T(8,128)}) fusion(pred[256,1280]{0,1:T(8,128)(4,1)} %fusion.28, bf16[256,16,128]{0,2,1:T(8,128)(2,1)S(1)} %bitcast.230, bf16[2,1280,256]{2,1,0:T(8,128)(2,1)S(1)} %constant_dynamic-update-slice_fusion), kind=kOutput, calls=%fused_computation.29 | convolution fusion | flops 340788480 | bytes 6164480 | tf_op jit(solution)/shard_map/sub | solution.py:26
  67.4 5.1 %exponential_reduce_fusion = (f32[4,256]{1,0:T(4,128)S(1)}, f32[4,256,1280]{1,2,0:T(8,128)}) fusion(pred[256,1280]{0,1:T(8,128)(4,1)} %fusion.28, bf16[256,16,128]{0,2,1:T(8,128)(2,1)S(1)} %bitcast.231, bf16[2,1280,256]{2,1,0:T(8,128)(2,1)S(1)} %constant_dynamic-update-slice_fusion), kind=kOutput, calls=%fused_computation.25 | convolution fusion | flops 340788480 | bytes 6164480 | tf_op jit(solution)/shard_map/sub | solution.py:26
  72.5 4.0 %fusion.23 = bf16[4,256,1280]{1,2,0:T(8,128)(2,1)S(1)} fusion(f32[4,256]{1,0:T(4,128)S(1)} %get-tuple-element.24, f32[4,256,1280]{1,2,0:T(8,128)} %get-tuple-element.25), kind=kLoop, calls=%fused_computation.50 | loop fusion | flops 2621440 | bytes 7868416 | tf_op jit(solution)/shard_map/convert_element_type | solution.py:28
  76.5 1.0 convolution_bitcast_fusion.3
  77.5 1.3 fusion.37
  78.8 1.1 fusion.15
  79.9 1.0 convolution_bitcast_fusion.7
  82.2 1.6 fusion.25
  83.8 1.0 convolution_bitcast_fusion.1
  84.8 1.3 fusion.39
  86.1 1.1 fusion.11
  87.3 1.0 convolution_bitcast_fusion.5
  89.5 1.4 fusion.24
  91.0 1.3 fusion.38
  92.2 1.0 fusion.18
  93.2 1.1 fusion.13
  94.4 1.2 slice-done
  95.6 1.0 slice-done.1
  96.7 1.4 fusion.26
  98.1 1.3 fusion.40
  99.4 1.0 fusion.17
  100.4 2.5 %fusion.9 = bf16[4,256,1280]{1,2,0:T(8,128)(2,1)S(1)} fusion(f32[4,256]{1,0:T(4,128)S(1)} %bitcast.242, f32[4,256]{1,0:T(4,128)S(1)} %get-tuple-element.18, f32[4,256,1280]{1,2,0:T(8,128)S(1)} %bitcast.221, bf16[2,1280,256]{2,1,0:T(8,128)(2,1)} %copy-done.5, bf16[256,16,128]{0,2,1:T(8,128)(2,1)} %bitcast.219), kind=kOutput, calls=%fused_computation.10 | convolution fusion | flops 340787200 | bytes 8462336 | tf_op jit(solution)/shard_map/rgd,ed->gre/dot_general | solution.py:31
  102.9 1.0 fusion.22
  104.0 1.0 fusion.20
  105.4 1.3 collective-permute-start.4
  106.7 1.3 collective-permute-start.7
  108.0 1.3 collective-permute-start.6
  109.3 1.3 collective-permute-start.5
  110.6 23.0 %collective-permute-done.4 = bf16[2,256,256]{1,2,0:T(8,128)(2,1)S(1)} collective-permute-done((bf16[2,256,256]{1,2,0:T(8,128)(2,1)S(1)}, bf16[2,256,256]{1,2,0:T(8,128)(2,1)S(1)}, u32[]{:S(2)}, u32[]{:S(2)}) %collective-permute-start.4) | collective-permute-done | bytes 262176 | tf_op jit(solution)/shard_map/ppermute | solution.py:16
  133.6 6.1 %collective-permute-done.5 = bf16[2,256,256]{1,2,0:T(8,128)(2,1)S(1)} collective-permute-done((bf16[2,256,256]{1,2,0:T(8,128)(2,1)S(1)}, bf16[2,256,256]{1,2,0:T(8,128)(2,1)S(1)}, u32[]{:S(2)}, u32[]{:S(2)}) %collective-permute-start.5) | collective-permute-done | bytes 262176 | tf_op jit(solution)/shard_map/ppermute | solution.py:16
  139.9 1.0 copy.188
  140.9 2.5 %fusion.44 = bf16[256,4,128]{0,2,1:T(8,128)(2,1)S(1)} fusion(bf16[4,256,1280]{1,2,0:T(8,128)(2,1)} %copy-done.2, bf16[2,1280,256]{2,1,0:T(8,128)(2,1)} %copy-done.5), kind=kOutput, calls=%fused_computation.83 | convolution fusion | flops 335806464 | bytes 3211264 | tf_op jit(solution)/shard_map/gre,ed->rgd/dot_general | solution.py:35
  143.5 3.1 %fusion.42 = bf16[256,4,128]{0,2,1:T(8,128)(2,1)} fusion(bf16[4,256,1280]{1,2,0:T(8,128)(2,1)} %copy-done.3, bf16[2,1280,256]{2,1,0:T(8,128)(2,1)} %copy-done.5), kind=kOutput, calls=%fused_computation.81 | convolution fusion | flops 335806464 | bytes 3211264 | tf_op jit(solution)/shard_map/gre,ed->rgd/dot_general | solution.py:35
  146.6 2.2 %fusion.43 = bf16[256,4,128]{0,2,1:T(8,128)(2,1)} fusion(bf16[4,256,1280]{1,2,0:T(8,128)(2,1)S(1)} %copy-done.1, bf16[2,1280,256]{2,1,0:T(8,128)(2,1)} %copy-done.5), kind=kOutput, calls=%fused_computation.82 | convolution fusion | flops 335806464 | bytes 3211264 | tf_op jit(solution)/shard_map/gre,ed->rgd/dot_general | solution.py:35
  148.8 43.8 %all-gather.3.cloned.1.call-done = f32[8,256,256]{2,1,0:T(8,128)} async-done(((f32[2,256,256]{2,1,0:T(8,128)}), f32[8,256,256]{2,1,0:T(8,128)}) %all-gather.3.cloned.1.call-update) | async-done | bytes 2097168 | tf_op jit(solution)/shard_map/all_gather | solution.py:97
  192.7 1.8 reduce_sum.89
  194.5 1.2 copy.190
  195.7 4.3 %all-to-all-start.1 = ((f32[2,256,256]{2,0,1:T(2,128)}), f32[2,256,256]{2,0,1:T(2,128)S(1)}, u32[]{:S(2)}, u32[]{:S(2)}) async-start(f32[2,256,256]{2,0,1:T(2,128)} %copy.190), calls=%async_computation.1 | async-start | bytes 1048576 | tf_op jit(solution)/shard_map/all_to_all | solution.py:98
  199.9 1.6 fusion.41
  201.7 1.4 copy.193
  203.1 4.7 %all-to-all-done.1 = f32[2,256,256]{2,0,1:T(2,128)S(1)} async-done(((f32[2,256,256]{2,0,1:T(2,128)}), f32[2,256,256]{2,0,1:T(2,128)S(1)}, u32[]{:S(2)}, u32[]{:S(2)}) %all-to-all-start.1) | async-done | bytes 524320 | tf_op jit(solution)/shard_map/all_to_all | solution.py:98
  207.8 0.8 copy.248
  (68 shorter events, 4.4 us)
Async XLA Ops:
  7.2 20.5 %copy-start.12 = (bf16[1,256,2048]{2,1,0:T(8,128)(2,1)S(1)}, bf16[1,256,2048]{2,1,0:T(8,128)(2,1)}, u32[]{:S(2)}) copy-start(bf16[1,256,2048]{2,1,0:T(8,128)(2,1)} %param.4) | copy-start | bytes 3145732
  9.6 11.6 %all-to-all-start = ((bf16[4,2,16384]{2,1,0:T(2,128)(2,1)}), bf16[4,2,16384]{2,1,0:T(2,128)(2,1)S(1)}, u32[]{:S(2)}, u32[]{:S(2)}) async-start(bf16[4,2,16384]{2,1,0:T(2,128)(2,1)} %reshape.106), calls=%async_computation | async-start | bytes 524288 | tf_op jit(solution)/shard_map/all_to_all | solution.py:47
  16.2 176.5 %all-gather.3.cloned.1.call-start = ((), (), s32[]{:S(2)}) async-start(), calls=%async_computation.2 | async-start | bytes 2621440 | tf_op jit(solution)/shard_map/all_gather | solution.py:97
  22.6 24.3 %collective-permute-start = (bf16[2,256,256]{2,1,0:T(8,128)(2,1)}, bf16[2,256,256]{2,1,0:T(8,128)(2,1)}, u32[]{:S(2)}, u32[]{:S(2)}) collective-permute-start(bf16[2,256,256]{2,1,0:T(8,128)(2,1)} %bitcast.2), channel_id=1, source_target_pairs={{0,16},{4,20},{8,24},{12,28},{16,32},{20,36},{24,40},{28,44},{32,4... | collective-permute-start | bytes 786440 | tf_op jit(solution)/shard_map/ppermute | solution.py:16
  28.2 71.2 %copy-start.4 = (bf16[1,256,2048]{1,2,0:T(8,128)(2,1)}, bf16[1,256,2048]{1,2,0:T(8,128)(2,1)S(1)}, u32[]{:S(2)}) copy-start(bf16[1,256,2048]{1,2,0:T(8,128)(2,1)S(1)} %copy.144) | copy-start | bytes 3145732
  28.2 20.7 %collective-permute-start.2 = (bf16[2,256,256]{2,1,0:T(8,128)(2,1)}, bf16[2,256,256]{2,1,0:T(8,128)(2,1)}, u32[]{:S(2)}, u32[]{:S(2)}) collective-permute-start(bf16[2,256,256]{2,1,0:T(8,128)(2,1)} %bitcast.2), channel_id=1, source_target_pairs={{0,8},{4,12},{8,16},{12,20},{16,24},{20,28},{24,32},{28,36},{32,40... | collective-permute-start | bytes 786440 | tf_op jit(solution)/shard_map/ppermute | solution.py:16
  32.4 15.5 %collective-permute-start.1 = (bf16[2,256,256]{2,1,0:T(8,128)(2,1)}, bf16[2,256,256]{2,1,0:T(8,128)(2,1)}, u32[]{:S(2)}, u32[]{:S(2)}) collective-permute-start(bf16[2,256,256]{2,1,0:T(8,128)(2,1)} %bitcast.2), channel_id=1, source_target_pairs={{0,12},{4,16},{8,20},{12,24},{16,28},{20,32},{24,36},{28,40},{32,4... | collective-permute-start | bytes 786440 | tf_op jit(solution)/shard_map/ppermute | solution.py:16
  40.7 46.5 %copy-start.6 = (bf16[1,256,2048]{1,2,0:T(8,128)(2,1)}, bf16[1,256,2048]{1,2,0:T(8,128)(2,1)S(1)}, u32[]{:S(2)}) copy-start(bf16[1,256,2048]{1,2,0:T(8,128)(2,1)S(1)} %copy.142) | copy-start | bytes 3145732
  44.3 6.6 %collective-permute-start.3 = (bf16[2,256,256]{2,1,0:T(8,128)(2,1)}, bf16[2,256,256]{2,1,0:T(8,128)(2,1)S(1)}, u32[]{:S(2)}, u32[]{:S(2)}) collective-permute-start(bf16[2,256,256]{2,1,0:T(8,128)(2,1)} %bitcast.2), channel_id=1, source_target_pairs={{0,4},{4,8},{8,12},{12,16},{16,20},{20,24},{24,28},{28,32},{32,36}... | collective-permute-start | bytes 786440 | tf_op jit(solution)/shard_map/ppermute | solution.py:16
  51.9 46.2 %copy-start.5 = (bf16[2,1280,256]{2,1,0:T(8,128)(2,1)}, bf16[2,1280,256]{2,1,0:T(8,128)(2,1)S(1)}, u32[]{:S(2)}) copy-start(bf16[2,1280,256]{2,1,0:T(8,128)(2,1)S(1)} %constant_dynamic-update-slice_fusion) | copy-start | bytes 3932164
  72.5 6.3 %slice-start.6 = ((s8[5242880]{0:T(1024)(128)(4,1)}), s8[4194304]{0:T(1024)(128)(4,1)S(1)}, s32[]{:S(2)}) async-start(s8[5242880]{0:T(1024)(128)(4,1)} %bitcast.226), calls=%async_computation.9 | async-start | bytes 8388608
  76.5 1.0 copy-start.11
  76.5 2.3 %slice-start.7 = ((s8[5242880]{0:T(1024)(128)(4,1)}), s8[1048576]{0:T(1024)(128)(4,1)S(1)}, s32[]{:S(2)}) async-start(s8[5242880]{0:T(1024)(128)(4,1)} %bitcast.226), calls=%async_computation.10 | async-start | bytes 2097152
  78.8 2.7 %slice-start.4 = ((s8[5242880]{0:T(1024)(128)(4,1)}), s8[4194304]{0:T(1024)(128)(4,1)S(1)}, s32[]{:S(2)}) async-start(s8[5242880]{0:T(1024)(128)(4,1)} %bitcast.224), calls=%async_computation.7 | async-start | bytes 8388608
  78.8 3.4 %slice-start.5 = ((s8[5242880]{0:T(1024)(128)(4,1)}), s8[1048576]{0:T(1024)(128)(4,1)S(1)}, s32[]{:S(2)}) async-start(s8[5242880]{0:T(1024)(128)(4,1)} %bitcast.224), calls=%async_computation.8 | async-start | bytes 2097152
  79.9 1.5 copy-start.2
  83.8 1.0 copy-start.10
  86.1 2.7 %slice-start.2 = ((s8[5242880]{0:T(1024)(128)(4,1)}), s8[4194304]{0:T(1024)(128)(4,1)S(1)}, s32[]{:S(2)}) async-start(s8[5242880]{0:T(1024)(128)(4,1)} %bitcast.222), calls=%async_computation.5 | async-start | bytes 8388608
  86.1 3.4 %slice-start.3 = ((s8[5242880]{0:T(1024)(128)(4,1)}), s8[1048576]{0:T(1024)(128)(4,1)S(1)}, s32[]{:S(2)}) async-start(s8[5242880]{0:T(1024)(128)(4,1)} %bitcast.222), calls=%async_computation.6 | async-start | bytes 2097152
  87.2 1.6 copy-start.3
  89.5 1.4 copy-start.9
  93.2 2.4 %slice-start = ((s8[5242880]{0:T(1024)(128)(4,1)}), s8[4194304]{0:T(1024)(128)(4,1)S(1)}, s32[]{:S(2)}) async-start(s8[5242880]{0:T(1024)(128)(4,1)} %bitcast.220), calls=%async_computation.3 | async-start | bytes 8388608
  93.2 3.4 %slice-start.1 = ((s8[5242880]{0:T(1024)(128)(4,1)}), s8[1048576]{0:T(1024)(128)(4,1)S(1)}, s32[]{:S(2)}) async-start(s8[5242880]{0:T(1024)(128)(4,1)} %bitcast.220), calls=%async_computation.4 | async-start | bytes 2097152
  94.4 8.5 %copy-start = (bf16[4,256,1280]{1,2,0:T(8,128)(2,1)}, bf16[4,256,1280]{1,2,0:T(8,128)(2,1)S(1)}, u32[]{:S(2)}) copy-start(bf16[4,256,1280]{1,2,0:T(8,128)(2,1)S(1)} %fusion.13) | copy-start | bytes 7864324
  96.7 1.4 copy-start.8
  100.4 2.6 %copy-start.7 = (bf16[1,256,2048]{1,2,0:T(8,128)(2,1)S(1)}, bf16[1,256,2048]{1,2,0:T(8,128)(2,1)}, u32[]{:S(2)}) copy-start(bf16[1,256,2048]{1,2,0:T(8,128)(2,1)} %copy-done.6) | copy-start | bytes 3145732
  105.4 28.2 %collective-permute-start.4 = (bf16[2,256,256]{1,2,0:T(8,128)(2,1)S(1)}, bf16[2,256,256]{1,2,0:T(8,128)(2,1)S(1)}, u32[]{:S(2)}, u32[]{:S(2)}) collective-permute-start(bf16[2,256,256]{1,2,0:T(8,128)(2,1)S(1)} %get-tuple-element.10), channel_id=1, source_target_pairs={{16,0},{20,4},{24,8},{28,12},{32,16},{36,20},{40,24},{44,28},{48,3... | collective-permute-start | bytes 786440 | tf_op jit(solution)/shard_map/ppermute | solution.py:16
  106.7 26.9 %collective-permute-start.7 = (bf16[2,256,256]{1,2,0:T(8,128)(2,1)S(1)}, bf16[2,256,256]{1,2,0:T(8,128)(2,1)S(1)}, u32[]{:S(2)}, u32[]{:S(2)}) collective-permute-start(bf16[2,256,256]{1,2,0:T(8,128)(2,1)S(1)} %get-tuple-element.11), channel_id=1, source_target_pairs={{4,0},{8,4},{12,8},{16,12},{20,16},{24,20},{28,24},{32,28},{36,32}... | collective-permute-start | bytes 786440 | tf_op jit(solution)/shard_map/ppermute | solution.py:16
  108.0 25.6 %collective-permute-start.6 = (bf16[2,256,256]{1,2,0:T(8,128)(2,1)S(1)}, bf16[2,256,256]{1,2,0:T(8,128)(2,1)S(1)}, u32[]{:S(2)}, u32[]{:S(2)}) collective-permute-start(bf16[2,256,256]{1,2,0:T(8,128)(2,1)S(1)} %get-tuple-element.12), channel_id=1, source_target_pairs={{8,0},{12,4},{16,8},{20,12},{24,16},{28,20},{32,24},{36,28},{40,32... | collective-permute-start | bytes 786440 | tf_op jit(solution)/shard_map/ppermute | solution.py:16
  109.3 30.4 %collective-permute-start.5 = (bf16[2,256,256]{1,2,0:T(8,128)(2,1)S(1)}, bf16[2,256,256]{1,2,0:T(8,128)(2,1)S(1)}, u32[]{:S(2)}, u32[]{:S(2)}) collective-permute-start(bf16[2,256,256]{1,2,0:T(8,128)(2,1)S(1)} %get-tuple-element.13), channel_id=1, source_target_pairs={{12,0},{16,4},{20,8},{24,12},{28,16},{32,20},{36,24},{40,28},{44,3... | collective-permute-start | bytes 786440 | tf_op jit(solution)/shard_map/ppermute | solution.py:16
  140.9 5.7 %copy-start.1 = (bf16[4,256,1280]{1,2,0:T(8,128)(2,1)S(1)}, bf16[4,256,1280]{1,2,0:T(8,128)(2,1)}, u32[]{:S(2)}) copy-start(bf16[4,256,1280]{1,2,0:T(8,128)(2,1)} %copy-done) | copy-start | bytes 7864324
  195.7 12.1 %all-to-all-start.1 = ((f32[2,256,256]{2,0,1:T(2,128)}), f32[2,256,256]{2,0,1:T(2,128)S(1)}, u32[]{:S(2)}, u32[]{:S(2)}) async-start(f32[2,256,256]{2,0,1:T(2,128)} %copy.190), calls=%async_computation.1 | async-start | bytes 1048576 | tf_op jit(solution)/shard_map/all_to_all | solution.py:98
  199.9 1.6 copy-start.13
  199.9 1.6 copy-start.14
Sparse Core Ops, SparseCore 0:
  141.1 51.5 all-gather.2
